TPU v7x, 256 devices: a whole 4x4x8 slice. The times are simulated.
256 devices in a mesh: ctx: 128 (over y, x, z), head: 2 (over core).
Axes of the slice: x: 4, y: 4, z: 8, core: 2. Of those that a mesh axis runs over, the one named last changes fastest.
Arguments:
- queries: bfloat16 [16384, 4096], P('ctx', 'head'), may hold values from -9 to 9
- key_rows: bfloat16 [16384, 4096], P('ctx', 'head'), may hold values from -9 to 9
- value_rows: bfloat16 [16384, 4096], P('ctx', 'head'), may hold values from -6 to 6
- offsets: int32 [3, 32], P(None, 'head'), may hold values from 0 to 3, as said below
- sublayer_norm_gain: float32 [4096], P('head'), may hold values from 0.25 to 1.75
- cotangent: bfloat16 [16384, 4096], P('ctx', 'head'), may hold values from -6 to 6
Outputs:
- normed: bfloat16 [16384, 4096], P('ctx', 'head')
- query_grad: bfloat16 [16384, 4096], P('ctx', 'head')
- key_grad: bfloat16 [16384, 4096], P('ctx', 'head')
- value_grad: bfloat16 [16384, 4096], P('ctx', 'head')
Inputs may be any that keep to these rules, and one draw needn't show every extreme that they name: Row l holds offsets of 0 to 2**l - 1, and each of these values belongs to exactly 32 / 2**l heads.
All inputs are finite; a program needn't handle non-finite values.
Results may differ from a plain program's by a relative error of at most 0.007.
Values may be sent and summed in bfloat16 or wider, within the bound.
No kernel may reach another device: no remote copies, remote signals or barrier semaphores. Data moves between devices by JAX's collectives and lax.ppermute only.
A program may use at most 192 MiB of HBM per device.

v0:
```python
from functools import reduce
import math

import jax
import jax.numpy as jnp
from jax import lax
from jax.sharding import PartitionSpec as P

SEG0 = 512


NEG_FILL = -1e30
EPSILON = 1e-05


def as_sent(x):
    return jax.tree.map(lambda a: a.astype(jnp.bfloat16) if a.dtype == jnp.float32 else a, x)


def from_partner(block, axis, stride):
    count = lax.axis_size(axis)
    route = []
    for low in range(count):
        high = low | 1 << stride
        if high != low and high < count:
            route += [(low, high), (high, low)]
    return lax.ppermute(block, axis, route)


def pick_rows(source, mask_table, stride):
    count = source.shape[0] // stride
    shaped = source.reshape((count, stride) + source.shape[1:])
    chosen = mask_table.reshape((1, stride, mask_table.shape[1]) + (1,) * (source.ndim - 2))
    return jnp.sum(jnp.where(chosen, shaped, jnp.zeros((), source.dtype)), axis=1)


def put_rows(picked, mask_table, stride, filler):
    chosen = mask_table.reshape((1, stride, mask_table.shape[1]) + (1,) * (picked.ndim - 2))
    spread = jnp.where(chosen, picked[:, None], jnp.asarray(filler, picked.dtype))
    return spread.reshape((picked.shape[0] * stride,) + picked.shape[1:])


def swap_keys(members, bit_num):
    return jax.tree.map(
        lambda part, own: part.astype(own.dtype),
        from_partner(as_sent(members), "ctx", bit_num),
        members,
    )


def swap_queries(members, bit_num):
    return jax.tree.map(
        lambda part, own: part.astype(own.dtype),
        from_partner(as_sent(members), "ctx", bit_num),
        members,
    )


def swap_stats(members, bit_num):
    return from_partner(members, "ctx", bit_num)


def doubling(members, group_bits, mover, ctx_index):
    for bit_num in range(group_bits):
        arrived = mover(members, bit_num)
        is_lower = ctx_index >> bit_num & 1 == 0
        members = tuple(
            (
                jnp.where(
                    is_lower,
                    jnp.concatenate([own_part, peer_part], 0),
                    jnp.concatenate([peer_part, own_part], 0),
                )
                for own_part, peer_part in zip(members, arrived)
            )
        )
    return members


def grad_block(
    query_seg, key_seg, value_seg, dout_seg, lse_seg, delta_seg, score_scale, want_query, want_keys
):
    lse_t = jnp.transpose(lse_seg, (0, 2, 1))[..., None]
    delta_t = jnp.transpose(delta_seg, (0, 2, 1))[..., None]
    scores = (
        jnp.einsum("sqhd,skhd->shqk", query_seg, key_seg, preferred_element_type=jnp.float32)
        * score_scale
    )
    probs = jnp.exp(scores - lse_t)
    dprobs = jnp.einsum("sqhd,skhd->shqk", dout_seg, value_seg, preferred_element_type=jnp.float32)
    dscores = (probs * (dprobs - delta_t)).astype(jnp.bfloat16)
    query_part = None
    key_part = None
    value_part = None
    if want_query:
        query_part = (
            jnp.einsum("shqk,skhd->sqhd", dscores, key_seg, preferred_element_type=jnp.float32)
            * score_scale
        )
    if want_keys:
        probs_half = probs.astype(jnp.bfloat16)
        key_part = (
            jnp.einsum("shqk,sqhd->skhd", dscores, query_seg, preferred_element_type=jnp.float32)
            * score_scale
        )
        value_part = jnp.einsum(
            "shqk,sqhd->skhd", probs_half, dout_seg, preferred_element_type=jnp.float32
        )
    return (query_part, key_part, value_part)


def on_device(queries, key_rows, value_rows, offsets, sublayer_norm_gain, cotangent):
    tok_rows = queries.shape[0]
    head_local = offsets.shape[1]
    head_size = queries.shape[1] // head_local
    level_count = offsets.shape[0]
    feature_total_count = lax.axis_size("head") * queries.shape[1]
    ctx_index = lax.axis_index("ctx")
    score_scale = 1.0 / math.sqrt(head_size)
    shape3 = (tok_rows, head_local, head_size)
    query_all = queries.reshape(shape3)
    key_all = key_rows.reshape(shape3)
    value_all = value_rows.reshape(shape3)

    def level_layout(level_num):
        stride = 2**level_num
        picked_rows = tok_rows // stride
        group_size = max(1, SEG0 * stride // tok_rows)
        group_bits = group_size.bit_length() - 1
        seg_count = max(1, picked_rows // SEG0)
        mask_table = jnp.arange(stride, dtype=jnp.int32)[:, None] == offsets[level_num][None, :]
        return (stride, picked_rows, group_bits, seg_count, mask_table)

    stored = []
    maxima = []
    totals = []
    partials = []
    for level_num in range(level_count):
        stride, picked_rows, group_bits, seg_count, mask_table = level_layout(level_num)
        query_sel = pick_rows(query_all, mask_table, stride)
        key_sel = pick_rows(key_all, mask_table, stride)
        value_sel = pick_rows(value_all, mask_table, stride)
        key_group, value_group = doubling((key_sel, value_sel), group_bits, swap_keys, ctx_index)
        stored.append((key_group, value_group))
        query_seg = query_sel.reshape(seg_count, -1, head_local, head_size)
        key_seg = key_group.reshape(seg_count, SEG0, head_local, head_size)
        value_seg = value_group.reshape(seg_count, SEG0, head_local, head_size)
        scores = (
            jnp.einsum("sqhd,skhd->shqk", query_seg, key_seg, preferred_element_type=jnp.float32)
            * score_scale
        )
        row_max = jnp.max(scores, axis=-1)
        weights = jnp.exp(scores - row_max[..., None])
        row_total = jnp.sum(weights, axis=-1)
        level_out = jnp.einsum(
            "shqk,skhd->sqhd",
            weights.astype(jnp.bfloat16),
            value_seg,
            preferred_element_type=jnp.float32,
        )
        flat_max = jnp.transpose(row_max, (0, 2, 1)).reshape(picked_rows, head_local)
        flat_total = jnp.transpose(row_total, (0, 2, 1)).reshape(picked_rows, head_local)
        maxima.append(put_rows(flat_max, mask_table, stride, NEG_FILL))
        totals.append(put_rows(flat_total, mask_table, stride, 0.0))
        partials.append(
            put_rows(level_out.reshape(picked_rows, head_local, head_size), mask_table, stride, 0.0)
        )
    top_max = reduce(jnp.maximum, maxima)
    factors = [jnp.exp(each_max - top_max) for each_max in maxima]
    total = factors[0] * totals[0]
    summed = factors[0][..., None] * partials[0]
    for level_num in range(1, level_count):
        total = total + factors[level_num] * totals[level_num]
        summed = summed + factors[level_num][..., None] * partials[level_num]
    attended = (summed / total[..., None]).astype(jnp.bfloat16)
    log_total = top_max + jnp.log(total)
    attended_rows_flattened = attended.reshape(tok_rows, -1).astype(jnp.float32)
    first_sum, second_sum = lax.psum(
        (
            jnp.sum(attended_rows_flattened, axis=1),
            jnp.sum(attended_rows_flattened * attended_rows_flattened, axis=1),
        ),
        "head",
    )
    feature_mean = first_sum / feature_total_count
    variance = second_sum / feature_total_count - feature_mean * feature_mean
    inverse_deviation = 1.0 / jnp.sqrt(variance + EPSILON)
    normalized_input = (attended_rows_flattened - feature_mean[:, None]) * inverse_deviation[
        :, None
    ]
    normed = (normalized_input * sublayer_norm_gain[None, :]).astype(jnp.bfloat16)
    normalized_gradient = cotangent.astype(jnp.float32) * sublayer_norm_gain[None, :]
    gradient_sum_first, gradient_sum_second = lax.psum(
        (
            jnp.sum(normalized_gradient, axis=1),
            jnp.sum(normalized_gradient * normalized_input, axis=1),
        ),
        "head",
    )
    attended_gradient = (
        (
            normalized_gradient
            - gradient_sum_first[:, None] / feature_total_count
            - normalized_input * gradient_sum_second[:, None] / feature_total_count
        )
        * inverse_deviation[:, None]
    ).astype(jnp.bfloat16)
    dout_all = attended_gradient.reshape(shape3)
    delta = jnp.sum(dout_all.astype(jnp.float32) * attended.astype(jnp.float32), axis=-1)
    query_acc = jnp.zeros(shape3, jnp.float32)
    key_acc = jnp.zeros(shape3, jnp.float32)
    value_acc = jnp.zeros(shape3, jnp.float32)
    for level_num in range(level_count):
        stride, picked_rows, group_bits, seg_count, mask_table = level_layout(level_num)
        query_sel = pick_rows(query_all, mask_table, stride)
        key_sel = pick_rows(key_all, mask_table, stride)
        value_sel = pick_rows(value_all, mask_table, stride)
        dout_sel = pick_rows(dout_all, mask_table, stride)
        lse_sel = pick_rows(log_total, mask_table, stride)
        delta_sel = pick_rows(delta, mask_table, stride)
        key_group, value_group = stored[level_num]
        query_seg = query_sel.reshape(seg_count, -1, head_local, head_size)
        dout_seg = dout_sel.reshape(seg_count, -1, head_local, head_size)
        lse_seg = lse_sel.reshape(seg_count, -1, head_local)
        delta_seg = delta_sel.reshape(seg_count, -1, head_local)
        key_seg = key_group.reshape(seg_count, SEG0, head_local, head_size)
        value_seg = value_group.reshape(seg_count, SEG0, head_local, head_size)
        query_part, unused_key, unused_value = grad_block(
            query_seg, key_seg, value_seg, dout_seg, lse_seg, delta_seg, score_scale, True, False
        )
        query_group, dout_group = doubling(
            (query_sel, dout_sel), group_bits, swap_queries, ctx_index
        )
        lse_group, delta_group = doubling((lse_sel, delta_sel), group_bits, swap_stats, ctx_index)
        unused_query, key_part, value_part = grad_block(
            query_group.reshape(seg_count, SEG0, head_local, head_size),
            key_sel.reshape(seg_count, -1, head_local, head_size),
            value_sel.reshape(seg_count, -1, head_local, head_size),
            dout_group.reshape(seg_count, SEG0, head_local, head_size),
            lse_group.reshape(seg_count, SEG0, head_local),
            delta_group.reshape(seg_count, SEG0, head_local),
            score_scale,
            False,
            True,
        )
        key_own = key_part.reshape(picked_rows, head_local, head_size)
        value_own = value_part.reshape(picked_rows, head_local, head_size)
        query_acc = query_acc + put_rows(
            query_part.reshape(picked_rows, head_local, head_size), mask_table, stride, 0.0
        )
        key_acc = key_acc + put_rows(key_own, mask_table, stride, 0.0)
        value_acc = value_acc + put_rows(value_own, mask_table, stride, 0.0)
    flat_shape = (tok_rows, head_local * head_size)
    query_grad = query_acc.astype(jnp.bfloat16).reshape(flat_shape)
    key_grad = key_acc.astype(jnp.bfloat16).reshape(flat_shape)
    value_grad = value_acc.astype(jnp.bfloat16).reshape(flat_shape)
    return (normed, query_grad, key_grad, value_grad)


def solution(mesh):
    in_specs = (
        P("ctx", "head"),
        P("ctx", "head"),
        P("ctx", "head"),
        P(None, "head"),
        P("head"),
        P("ctx", "head"),
    )
    out_specs = (P("ctx", "head"), P("ctx", "head"), P("ctx", "head"), P("ctx", "head"))
    return jax.shard_map(
        on_device, mesh=mesh, in_specs=in_specs, out_specs=out_specs, check_vma=False
    )
```

profile of v0, /device:TPU:2, one launch (start us, length us, event | category | flops | bytes accessed | tf_op | source)
XLA Modules:
  0.0 886.1 jit_solution(13964842547562466004)
XLA Ops:
  18.3 4.6 collective-permute-done.14
  28.8 10.8 %collective-permute-done.38 = bf16[32,16,128]{2,1,0:T(8,128)(2,1)S(1)} collective-permute-done((bf16[32,16,128]{2,1,0:T(8,128)(2,1)S(1)}, bf16[32,16,128]{2,1,0:T(8,128)(2,1)S(1)}, u32[]{:S(2)}, u32[]{:S(2)}) %collective-permute-start.38) | collective-permute-done | bytes 131104 | tf_op jit(solution)/shard_map/ppermute | solution.py:27
  41.6 3.4 collective-permute-start.15
  47.5 19.3 %collective-permute-done.26 = bf16[64,16,128]{2,1,0:T(8,128)(2,1)S(1)} collective-permute-done((bf16[64,16,128]{2,1,0:T(8,128)(2,1)S(1)}, bf16[64,16,128]{2,1,0:T(8,128)(2,1)S(1)}, u32[]{:S(2)}, u32[]{:S(2)}) %collective-permute-start.26) | collective-permute-done | bytes 262176 | tf_op jit(solution)/shard_map/ppermute | solution.py:27
  72.3 10.2 %collective-permute-done.39 = bf16[64,16,128]{2,1,0:T(8,128)(2,1)S(1)} collective-permute-done((bf16[64,16,128]{2,1,0:T(8,128)(2,1)S(1)}, bf16[64,16,128]{2,1,0:T(8,128)(2,1)S(1)}, u32[]{:S(2)}, u32[]{:S(2)}) %collective-permute-start.39) | collective-permute-done | bytes 262176 | tf_op jit(solution)/shard_map/ppermute | solution.py:27
  82.6 3.2 collective-permute-start.27
  88.9 5.1 collective-permute-done.18
  94.0 5.0 collective-permute-start.16
  100.4 71.9 %collective-permute-done.3 = bf16[128,16,128]{2,1,0:T(8,128)(2,1)S(1)} collective-permute-done((bf16[128,16,128]{2,1,0:T(8,128)(2,1)S(1)}, bf16[128,16,128]{2,1,0:T(8,128)(2,1)S(1)}, u32[]{:S(2)}, u32[]{:S(2)}) %collective-permute-start.3) | collective-permute-done | bytes 524320 | tf_op jit(solution)/shard_map/ppermute | solution.py:27
  172.3 4.5 collective-permute-start.7
  177.0 18.0 %collective-permute-done.12 = bf16[128,16,128]{2,1,0:T(8,128)(2,1)S(1)} collective-permute-done((bf16[128,16,128]{2,1,0:T(8,128)(2,1)S(1)}, bf16[128,16,128]{2,1,0:T(8,128)(2,1)S(1)}, u32[]{:S(2)}, u32[]{:S(2)}) %collective-permute-start.12) | collective-permute-done | bytes 524320 | tf_op jit(solution)/shard_map/ppermute | solution.py:27
  195.0 4.5 collective-permute-start.40
  199.7 18.0 %collective-permute-done.27 = bf16[128,16,128]{2,1,0:T(8,128)(2,1)S(1)} collective-permute-done((bf16[128,16,128]{2,1,0:T(8,128)(2,1)S(1)}, bf16[128,16,128]{2,1,0:T(8,128)(2,1)S(1)}, u32[]{:S(2)}, u32[]{:S(2)}) %collective-permute-start.27) | collective-permute-done | bytes 524320 | tf_op jit(solution)/shard_map/ppermute | solution.py:27
  218.9 2.9 collective-permute-start.19
  223.0 4.5 collective-permute-start.4
  231.2 165.8 %collective-permute-done.1 = bf16[256,16,128]{0,2,1:T(8,128)(2,1)S(1)} collective-permute-done((bf16[256,16,128]{0,2,1:T(8,128)(2,1)S(1)}, bf16[256,16,128]{0,2,1:T(8,128)(2,1)S(1)}, u32[]{:S(2)}, u32[]{:S(2)}) %collective-permute-start.1) | collective-permute-done | bytes 1048608 | tf_op jit(solution)/shard_map/ppermute | solution.py:27
  397.0 4.5 collective-permute-start.28
  406.3 57.1 %collective-permute-done.19 = bf16[256,16,128]{0,2,1:T(8,128)(2,1)} collective-permute-done((bf16[256,16,128]{0,2,1:T(8,128)(2,1)}, bf16[256,16,128]{0,2,1:T(8,128)(2,1)}, u32[]{:S(2)}, u32[]{:S(2)}) %collective-permute-start.19) | collective-permute-done | bytes 1048608 | tf_op jit(solution)/shard_map/ppermute | solution.py:27
  464.0 5.2 fusion.159
  492.4 19.9 %collective-permute-done.8 = bf16[256,16,128]{2,1,0:T(8,128)(2,1)} collective-permute-done((bf16[256,16,128]{2,1,0:T(8,128)(2,1)}, bf16[256,16,128]{2,1,0:T(8,128)(2,1)}, u32[]{:S(2)}, u32[]{:S(2)}) %collective-permute-start.8) | collective-permute-done | bytes 1048608 | tf_op jit(solution)/shard_map/ppermute | solution.py:27
  524.7 6.8 convert_reduce_fusion
  542.4 2.9 copy.329
  551.4 5.3 fusion.138
  556.8 3.0 all-reduce
  608.1 4.8 fusion.97
  612.9 4.7 fusion.79
  621.0 7.4 fusion.72
  641.9 3.9 collective-permute-done.29
  647.4 3.0 collective-permute-done.51
  651.9 3.1 collective-permute-done.43
  655.6 3.0 collective-permute-start.36
  661.1 26.5 %collective-permute-start.52 = (f32[128,16]{0,1:T(8,128)S(1)}, f32[128,16]{0,1:T(8,128)S(1)}, u32[]{:S(2)}, u32[]{:S(2)}) collective-permute-start(f32[128,16]{0,1:T(8,128)S(1)} %maximum_select_fusion.63), channel_id=1, source_target_pairs={{0,8},{8,0},{2,10},{10,2},{4,12},{12,4},{6,14},{14,6},{16,24},{24,... | collective-permute-start | bytes 24584 | tf_op jit(solution)/shard_map/ppermute | solution.py:27
  687.6 3.8 collective-permute-start.44
  692.2 3.1 collective-permute-done.44
  700.5 4.1 collective-permute-start.31
  710.6 3.0 collective-permute-start.47
  719.5 30.5 %collective-permute-done.47 = bf16[64,16,128]{2,1,0:T(8,128)(2,1)S(1)} collective-permute-done((bf16[64,16,128]{2,1,0:T(8,128)(2,1)S(1)}, bf16[64,16,128]{2,1,0:T(8,128)(2,1)S(1)}, u32[]{:S(2)}, u32[]{:S(2)}) %collective-permute-start.47) | collective-permute-done | bytes 262176 | tf_op jit(solution)/shard_map/ppermute | solution.py:27
  750.1 3.1 collective-permute-start.48
  753.2 3.0 fusion.66
  756.2 38.2 %collective-permute-done.33 = bf16[128,16,128]{2,1,0:T(8,128)(2,1)S(1)} collective-permute-done((bf16[128,16,128]{2,1,0:T(8,128)(2,1)S(1)}, bf16[128,16,128]{2,1,0:T(8,128)(2,1)S(1)}, u32[]{:S(2)}, u32[]{:S(2)}) %collective-permute-start.33) | collective-permute-done | bytes 524320 | tf_op jit(solution)/shard_map/ppermute | solution.py:27
  795.5 3.8 collective-permute-start.34
  801.0 6.9 convolution_multiply_fusion
  810.4 5.8 fusion.3
  818.8 35.0 %collective-permute-done.34 = bf16[256,16,128]{2,1,0:T(8,128)(2,1)} collective-permute-done((bf16[256,16,128]{2,1,0:T(8,128)(2,1)}, bf16[256,16,128]{2,1,0:T(8,128)(2,1)}, u32[]{:S(2)}, u32[]{:S(2)}) %collective-permute-start.34) | collective-permute-done | bytes 1048608 | tf_op jit(solution)/shard_map/ppermute | solution.py:27
  853.8 3.9 maximum_select_fusion.9
  857.7 5.4 fusion.85
  872.8 4.5 fusion.109
  881.8 3.8 fusion.119
  (372 shorter events, 213.0 us)
Async XLA Ops:
  5.2 36.4 %collective-permute-start.2 = (bf16[64,16,128]{2,1,0:T(8,128)(2,1)S(1)}, bf16[64,16,128]{2,1,0:T(8,128)(2,1)}, u32[]{:S(2)}, u32[]{:S(2)}) collective-permute-start(bf16[64,16,128]{2,1,0:T(8,128)(2,1)S(1)} %get-tuple-element.13), channel_id=1, source_target_pairs={{0,2},{2,0},{4,6},{6,4},{8,10},{10,8},{12,14},{14,12},{16,18},{18,... | collective-permute-start | bytes 786440 | tf_op jit(solution)/shard_map/ppermute | solution.py:27
  7.1 39.0 %collective-permute-start.11 = (bf16[64,16,128]{2,1,0:T(8,128)(2,1)}, bf16[64,16,128]{2,1,0:T(8,128)(2,1)}, u32[]{:S(2)}, u32[]{:S(2)}) collective-permute-start(bf16[64,16,128]{2,1,0:T(8,128)(2,1)} %get-tuple-element.12), channel_id=1, source_target_pairs={{0,2},{2,0},{4,6},{6,4},{8,10},{10,8},{12,14},{14,12},{16,18},{18,... | collective-permute-start | bytes 786440 | tf_op jit(solution)/shard_map/ppermute | solution.py:27
  8.6 14.3 %collective-permute-start.14 = (bf16[32,16,128]{2,1,0:T(8,128)(2,1)}, bf16[32,16,128]{2,1,0:T(8,128)(2,1)}, u32[]{:S(2)}, u32[]{:S(2)}) collective-permute-start(bf16[32,16,128]{2,1,0:T(8,128)(2,1)} %get-tuple-element.15), channel_id=1, source_target_pairs={{0,2},{2,0},{4,6},{6,4},{8,10},{10,8},{12,14},{14,12},{16,18},{18,... | collective-permute-start | bytes 393224 | tf_op jit(solution)/shard_map/ppermute | solution.py:27
  10.5 15.5 %collective-permute-start.5 = (bf16[32,16,128]{2,1,0:T(8,128)(2,1)}, bf16[32,16,128]{2,1,0:T(8,128)(2,1)}, u32[]{:S(2)}, u32[]{:S(2)}) collective-permute-start(bf16[32,16,128]{2,1,0:T(8,128)(2,1)} %get-tuple-element.16), channel_id=1, source_target_pairs={{0,2},{2,0},{4,6},{6,4},{8,10},{10,8},{12,14},{14,12},{16,18},{18,... | collective-permute-start | bytes 393224 | tf_op jit(solution)/shard_map/ppermute | solution.py:27
  13.1 69.5 %collective-permute-start = (bf16[128,16,128]{0,2,1:T(8,128)(2,1)S(1)}, bf16[128,16,128]{0,2,1:T(8,128)(2,1)}, u32[]{:S(2)}, u32[]{:S(2)}) collective-permute-start(bf16[128,16,128]{0,2,1:T(8,128)(2,1)S(1)} %get-tuple-element.45), channel_id=1, source_target_pairs={{0,2},{2,0},{4,6},{6,4},{8,10},{10,8},{12,14},{14,12},{16,18},{18,... | collective-permute-start | bytes 1572872 | tf_op jit(solution)/shard_map/ppermute | solution.py:27
  22.9 16.7 %collective-permute-start.38 = (bf16[32,16,128]{2,1,0:T(8,128)(2,1)S(1)}, bf16[32,16,128]{2,1,0:T(8,128)(2,1)S(1)}, u32[]{:S(2)}, u32[]{:S(2)}) collective-permute-start(bf16[32,16,128]{2,1,0:T(8,128)(2,1)S(1)} %get-tuple-element.17), channel_id=1, source_target_pairs={{0,2},{2,0},{4,6},{6,4},{8,10},{10,8},{12,14},{14,12},{16,18},{18,... | collective-permute-start | bytes 393224 | tf_op jit(solution)/shard_map/ppermute | solution.py:27
  26.0 61.4 %collective-permute-start.9 = (bf16[128,16,128]{0,2,1:T(8,128)(2,1)S(1)}, bf16[128,16,128]{0,2,1:T(8,128)(2,1)S(1)}, u32[]{:S(2)}, u32[]{:S(2)}) collective-permute-start(bf16[128,16,128]{0,2,1:T(8,128)(2,1)S(1)} %get-tuple-element.44), channel_id=1, source_target_pairs={{0,2},{2,0},{4,6},{6,4},{8,10},{10,8},{12,14},{14,12},{16,18},{18,... | collective-permute-start | bytes 1572872 | tf_op jit(solution)/shard_map/ppermute | solution.py:27
  39.6 27.1 %collective-permute-start.26 = (bf16[64,16,128]{2,1,0:T(8,128)(2,1)S(1)}, bf16[64,16,128]{2,1,0:T(8,128)(2,1)S(1)}, u32[]{:S(2)}, u32[]{:S(2)}) collective-permute-start(bf16[64,16,128]{2,1,0:T(8,128)(2,1)S(1)} %get-tuple-element.14), channel_id=1, source_target_pairs={{0,2},{2,0},{4,6},{6,4},{8,10},{10,8},{12,14},{14,12},{16,18},{18,... | collective-permute-start | bytes 786440 | tf_op jit(solution)/shard_map/ppermute | solution.py:27
  41.6 27.8 %collective-permute-start.15 = (bf16[64,16,128]{2,1,0:T(8,128)(2,1)S(1)}, bf16[64,16,128]{2,1,0:T(8,128)(2,1)S(1)}, u32[]{:S(2)}, u32[]{:S(2)}) collective-permute-start(bf16[64,16,128]{2,1,0:T(8,128)(2,1)S(1)} %maximum_select_fusion.43), channel_id=1, source_target_pairs={{0,4},{4,0},{2,6},{6,2},{8,12},{12,8},{10,14},{14,10},{16,20},{20,... | collective-permute-start | bytes 786440 | tf_op jit(solution)/shard_map/ppermute | solution.py:27
  46.1 26.0 %collective-permute-start.6 = (bf16[64,16,128]{2,1,0:T(8,128)(2,1)S(1)}, bf16[64,16,128]{2,1,0:T(8,128)(2,1)S(1)}, u32[]{:S(2)}, u32[]{:S(2)}) collective-permute-start(bf16[64,16,128]{2,1,0:T(8,128)(2,1)S(1)} %maximum_select_fusion.42), channel_id=1, source_target_pairs={{0,4},{4,0},{2,6},{6,2},{8,12},{12,8},{10,14},{14,10},{16,20},{20,... | collective-permute-start | bytes 786440 | tf_op jit(solution)/shard_map/ppermute | solution.py:27
  66.8 15.7 %collective-permute-start.39 = (bf16[64,16,128]{2,1,0:T(8,128)(2,1)S(1)}, bf16[64,16,128]{2,1,0:T(8,128)(2,1)S(1)}, u32[]{:S(2)}, u32[]{:S(2)}) collective-permute-start(bf16[64,16,128]{2,1,0:T(8,128)(2,1)S(1)} %maximum_select_fusion.44), channel_id=1, source_target_pairs={{0,4},{4,0},{2,6},{6,2},{8,12},{12,8},{10,14},{14,10},{16,20},{20,... | collective-permute-start | bytes 786440 | tf_op jit(solution)/shard_map/ppermute | solution.py:27
  69.4 24.6 %collective-permute-start.18 = (bf16[128,16,128]{0,2,1:T(8,128)(2,1)S(1)}, bf16[128,16,128]{0,2,1:T(8,128)(2,1)S(1)}, u32[]{:S(2)}, u32[]{:S(2)}) collective-permute-start(bf16[128,16,128]{0,2,1:T(8,128)(2,1)S(1)} %copy-done.27), channel_id=1, source_target_pairs={{0,2},{2,0},{4,6},{6,4},{8,10},{10,8},{12,14},{14,12},{16,18},{18,... | collective-permute-start | bytes 1572872 | tf_op jit(solution)/shard_map/ppermute | solution.py:27
  72.1 100.2 %collective-permute-start.3 = (bf16[128,16,128]{2,1,0:T(8,128)(2,1)S(1)}, bf16[128,16,128]{2,1,0:T(8,128)(2,1)S(1)}, u32[]{:S(2)}, u32[]{:S(2)}) collective-permute-start(bf16[128,16,128]{2,1,0:T(8,128)(2,1)S(1)} %maximum_select_fusion.24), channel_id=1, source_target_pairs={{0,4},{4,0},{2,6},{6,2},{8,12},{12,8},{10,14},{14,10},{16,20},{20,... | collective-permute-start | bytes 1572872 | tf_op jit(solution)/shard_map/ppermute | solution.py:27
  82.5 112.5 %collective-permute-start.12 = (bf16[128,16,128]{2,1,0:T(8,128)(2,1)S(1)}, bf16[128,16,128]{2,1,0:T(8,128)(2,1)S(1)}, u32[]{:S(2)}, u32[]{:S(2)}) collective-permute-start(bf16[128,16,128]{2,1,0:T(8,128)(2,1)S(1)} %maximum_select_fusion.26), channel_id=1, source_target_pairs={{0,4},{4,0},{2,6},{6,2},{8,12},{12,8},{10,14},{14,10},{16,20},{20,... | collective-permute-start | bytes 1572872 | tf_op jit(solution)/shard_map/ppermute | solution.py:27
  82.6 135.1 %collective-permute-start.27 = (bf16[128,16,128]{2,1,0:T(8,128)(2,1)S(1)}, bf16[128,16,128]{2,1,0:T(8,128)(2,1)S(1)}, u32[]{:S(2)}, u32[]{:S(2)}) collective-permute-start(bf16[128,16,128]{2,1,0:T(8,128)(2,1)S(1)} %maximum_select_fusion.28), channel_id=1, source_target_pairs={{0,4},{4,0},{2,6},{6,2},{8,12},{12,8},{10,14},{14,10},{16,20},{20,... | collective-permute-start | bytes 1572872 | tf_op jit(solution)/shard_map/ppermute | solution.py:27
  87.4 309.6 %collective-permute-start.1 = (bf16[256,16,128]{0,2,1:T(8,128)(2,1)S(1)}, bf16[256,16,128]{0,2,1:T(8,128)(2,1)S(1)}, u32[]{:S(2)}, u32[]{:S(2)}) collective-permute-start(bf16[256,16,128]{0,2,1:T(8,128)(2,1)S(1)} %maximum_select_fusion.12), channel_id=1, source_target_pairs={{0,4},{4,0},{2,6},{6,2},{8,12},{12,8},{10,14},{14,10},{16,20},{20,... | collective-permute-start | bytes 3145736 | tf_op jit(solution)/shard_map/ppermute | solution.py:27
  94.0 124.9 %collective-permute-start.16 = (bf16[128,16,128]{2,1,0:T(8,128)(2,1)S(1)}, bf16[128,16,128]{2,1,0:T(8,128)(2,1)S(1)}, u32[]{:S(2)}, u32[]{:S(2)}) collective-permute-start(bf16[128,16,128]{2,1,0:T(8,128)(2,1)S(1)} %maximum_select_fusion.27), channel_id=1, source_target_pairs={{0,8},{8,0},{2,10},{10,2},{4,12},{12,4},{6,14},{14,6},{16,24},{24,... | collective-permute-start | bytes 1572872 | tf_op jit(solution)/shard_map/ppermute | solution.py:27
  172.3 50.7 %collective-permute-start.7 = (bf16[128,16,128]{2,1,0:T(8,128)(2,1)S(1)}, bf16[128,16,128]{2,1,0:T(8,128)(2,1)S(1)}, u32[]{:S(2)}, u32[]{:S(2)}) collective-permute-start(bf16[128,16,128]{2,1,0:T(8,128)(2,1)S(1)} %maximum_select_fusion.25), channel_id=1, source_target_pairs={{0,8},{8,0},{2,10},{10,2},{4,12},{12,4},{6,14},{14,6},{16,24},{24,... | collective-permute-start | bytes 1572872 | tf_op jit(solution)/shard_map/ppermute | solution.py:27
  195.0 33.6 %collective-permute-start.40 = (bf16[128,16,128]{2,1,0:T(8,128)(2,1)S(1)}, bf16[128,16,128]{2,1,0:T(8,128)(2,1)S(1)}, u32[]{:S(2)}, u32[]{:S(2)}) collective-permute-start(bf16[128,16,128]{2,1,0:T(8,128)(2,1)S(1)} %maximum_select_fusion.30), channel_id=1, source_target_pairs={{0,8},{8,0},{2,10},{10,2},{4,12},{12,4},{6,14},{14,6},{16,24},{24,... | collective-permute-start | bytes 1572872 | tf_op jit(solution)/shard_map/ppermute | solution.py:27
  217.7 307.0 %collective-permute-start.10 = (bf16[256,16,128]{0,2,1:T(8,128)(2,1)}, bf16[256,16,128]{0,2,1:T(8,128)(2,1)}, u32[]{:S(2)}, u32[]{:S(2)}) collective-permute-start(bf16[256,16,128]{0,2,1:T(8,128)(2,1)} %maximum_select_fusion.15), channel_id=1, source_target_pairs={{0,4},{4,0},{2,6},{6,2},{8,12},{12,8},{10,14},{14,10},{16,20},{20,... | collective-permute-start | bytes 3145736 | tf_op jit(solution)/shard_map/ppermute | solution.py:27
  218.9 244.6 %collective-permute-start.19 = (bf16[256,16,128]{0,2,1:T(8,128)(2,1)}, bf16[256,16,128]{0,2,1:T(8,128)(2,1)}, u32[]{:S(2)}, u32[]{:S(2)}) collective-permute-start(bf16[256,16,128]{0,2,1:T(8,128)(2,1)} %maximum_select_fusion.18), channel_id=1, source_target_pairs={{0,4},{4,0},{2,6},{6,2},{8,12},{12,8},{10,14},{14,10},{16,20},{20,... | collective-permute-start | bytes 3145736 | tf_op jit(solution)/shard_map/ppermute | solution.py:27
  223.0 246.2 %collective-permute-start.4 = (bf16[256,16,128]{2,1,0:T(8,128)(2,1)S(1)}, bf16[256,16,128]{2,1,0:T(8,128)(2,1)}, u32[]{:S(2)}, u32[]{:S(2)}) collective-permute-start(bf16[256,16,128]{2,1,0:T(8,128)(2,1)S(1)} %maximum_select_fusion.13), channel_id=1, source_target_pairs={{0,8},{8,0},{2,10},{10,2},{4,12},{12,4},{6,14},{14,6},{16,24},{24,... | collective-permute-start | bytes 3145736 | tf_op jit(solution)/shard_map/ppermute | solution.py:27
  228.7 244.1 %collective-permute-start.13 = (bf16[256,16,128]{2,1,0:T(8,128)(2,1)S(1)}, bf16[256,16,128]{2,1,0:T(8,128)(2,1)}, u32[]{:S(2)}, u32[]{:S(2)}) collective-permute-start(bf16[256,16,128]{2,1,0:T(8,128)(2,1)S(1)} %maximum_select_fusion.16), channel_id=1, source_target_pairs={{0,8},{8,0},{2,10},{10,2},{4,12},{12,4},{6,14},{14,6},{16,24},{24,... | collective-permute-start | bytes 3145736 | tf_op jit(solution)/shard_map/ppermute | solution.py:27
  397.0 85.4 %collective-permute-start.28 = (bf16[256,16,128]{2,1,0:T(8,128)(2,1)}, bf16[256,16,128]{2,1,0:T(8,128)(2,1)}, u32[]{:S(2)}, u32[]{:S(2)}) collective-permute-start(bf16[256,16,128]{2,1,0:T(8,128)(2,1)} %maximum_select_fusion.20), channel_id=1, source_target_pairs={{0,8},{8,0},{2,10},{10,2},{4,12},{12,4},{6,14},{14,6},{16,24},{24,... | collective-permute-start | bytes 3145736 | tf_op jit(solution)/shard_map/ppermute | solution.py:27
  463.5 26.3 %collective-permute-start.17 = (bf16[256,16,128]{2,1,0:T(8,128)(2,1)}, bf16[256,16,128]{2,1,0:T(8,128)(2,1)}, u32[]{:S(2)}, u32[]{:S(2)}) collective-permute-start(bf16[256,16,128]{2,1,0:T(8,128)(2,1)} %maximum_select_fusion.17), channel_id=1, source_target_pairs={{0,16},{16,0},{2,18},{18,2},{4,20},{20,4},{6,22},{22,6},{8,24},{24... | collective-permute-start | bytes 3145736 | tf_op jit(solution)/shard_map/ppermute | solution.py:27
  469.2 43.1 %collective-permute-start.8 = (bf16[256,16,128]{2,1,0:T(8,128)(2,1)}, bf16[256,16,128]{2,1,0:T(8,128)(2,1)}, u32[]{:S(2)}, u32[]{:S(2)}) collective-permute-start(bf16[256,16,128]{2,1,0:T(8,128)(2,1)} %maximum_select_fusion.14), channel_id=1, source_target_pairs={{0,16},{16,0},{2,18},{18,2},{4,20},{20,4},{6,22},{22,6},{8,24},{24... | collective-permute-start | bytes 3145736 | tf_op jit(solution)/shard_map/ppermute | solution.py:27
  472.8 144.9 %collective-permute-start.41 = (bf16[256,16,128]{2,1,0:T(8,128)(2,1)}, bf16[256,16,128]{2,1,0:T(8,128)(2,1)}, u32[]{:S(2)}, u32[]{:S(2)}) collective-permute-start(bf16[256,16,128]{2,1,0:T(8,128)(2,1)} %maximum_select_fusion.22), channel_id=1, source_target_pairs={{0,16},{16,0},{2,18},{18,2},{4,20},{20,4},{6,22},{22,6},{8,24},{24... | collective-permute-start | bytes 3145736 | tf_op jit(solution)/shard_map/ppermute | solution.py:27
  581.5 52.4 %collective-permute-start.50 = (f32[32,16]{1,0:T(8,128)}, f32[32,16]{1,0:T(8,128)}, u32[]{:S(2)}, u32[]{:S(2)}) collective-permute-start(f32[32,16]{1,0:T(8,128)} %get-tuple-element.11), channel_id=1, source_target_pairs={{0,2},{2,0},{4,6},{6,4},{8,10},{10,8},{12,14},{14,12},{16,18},{18,... | collective-permute-start | bytes 6152 | tf_op jit(solution)/shard_map/ppermute | solution.py:27
  583.0 54.4 %collective-permute-start.42 = (f32[32,16]{1,0:T(8,128)}, f32[32,16]{1,0:T(8,128)}, u32[]{:S(2)}, u32[]{:S(2)}) collective-permute-start(f32[32,16]{1,0:T(8,128)} %get-tuple-element.10), channel_id=1, source_target_pairs={{0,2},{2,0},{4,6},{6,4},{8,10},{10,8},{12,14},{14,12},{16,18},{18,... | collective-permute-start | bytes 6152 | tf_op jit(solution)/shard_map/ppermute | solution.py:27
  603.2 112.4 %collective-permute-start.32 = (bf16[64,16,128]{2,1,0:T(8,128)(2,1)}, bf16[64,16,128]{2,1,0:T(8,128)(2,1)}, u32[]{:S(2)}, u32[]{:S(2)}) collective-permute-start(bf16[64,16,128]{2,1,0:T(8,128)(2,1)} %select_reduce_fusion.1), channel_id=1, source_target_pairs={{0,2},{2,0},{4,6},{6,4},{8,10},{10,8},{12,14},{14,12},{16,18},{18,... | collective-permute-start | bytes 786440 | tf_op jit(solution)/shard_map/ppermute | solution.py:27
  603.3 106.2 %collective-permute-start.46 = (bf16[32,16,128]{2,1,0:T(8,128)(2,1)S(1)}, bf16[32,16,128]{2,1,0:T(8,128)(2,1)}, u32[]{:S(2)}, u32[]{:S(2)}) collective-permute-start(bf16[32,16,128]{2,1,0:T(8,128)(2,1)S(1)} %select_reduce_fusion), channel_id=1, source_target_pairs={{0,2},{2,0},{4,6},{6,4},{8,10},{10,8},{12,14},{14,12},{16,18},{18,... | collective-permute-start | bytes 393224 | tf_op jit(solution)/shard_map/ppermute | solution.py:27
  617.7 96.0 %collective-permute-start.22 = (bf16[128,16,128]{0,2,1:T(8,128)(2,1)S(1)}, bf16[128,16,128]{0,2,1:T(8,128)(2,1)}, u32[]{:S(2)}, u32[]{:S(2)}) collective-permute-start(bf16[128,16,128]{0,2,1:T(8,128)(2,1)S(1)} %copy-done.18), channel_id=1, source_target_pairs={{0,2},{2,0},{4,6},{6,4},{8,10},{10,8},{12,14},{14,12},{16,18},{18,... | collective-permute-start | bytes 1572872 | tf_op jit(solution)/shard_map/ppermute | solution.py:27
  633.9 21.7 %collective-permute-start.24 = (f32[128,16]{0,1:T(8,128)}, f32[128,16]{0,1:T(8,128)S(1)}, u32[]{:S(2)}, u32[]{:S(2)}) collective-permute-start(f32[128,16]{0,1:T(8,128)} %broadcast_select_fusion.8), channel_id=1, source_target_pairs={{0,2},{2,0},{4,6},{6,4},{8,10},{10,8},{12,14},{14,12},{16,18},{18,... | collective-permute-start | bytes 24584 | tf_op jit(solution)/shard_map/ppermute | solution.py:27
  655.6 5.5 collective-permute-start.36
  659.4 28.3 %collective-permute-start.30 = (f32[128,16]{0,1:T(8,128)S(1)}, f32[128,16]{0,1:T(8,128)S(1)}, u32[]{:S(2)}, u32[]{:S(2)}) collective-permute-start(f32[128,16]{0,1:T(8,128)S(1)} %maximum_select_fusion.58), channel_id=1, source_target_pairs={{0,4},{4,0},{2,6},{6,2},{8,12},{12,8},{10,14},{14,10},{16,20},{20,... | collective-permute-start | bytes 24584 | tf_op jit(solution)/shard_map/ppermute | solution.py:27
  661.1 30.3 %collective-permute-start.52 = (f32[128,16]{0,1:T(8,128)S(1)}, f32[128,16]{0,1:T(8,128)S(1)}, u32[]{:S(2)}, u32[]{:S(2)}) collective-permute-start(f32[128,16]{0,1:T(8,128)S(1)} %maximum_select_fusion.63), channel_id=1, source_target_pairs={{0,8},{8,0},{2,10},{10,2},{4,12},{12,4},{6,14},{14,6},{16,24},{24,... | collective-permute-start | bytes 24584 | tf_op jit(solution)/shard_map/ppermute | solution.py:27
  687.6 7.6 collective-permute-start.44
  691.4 6.7 collective-permute-start.25
  698.1 7.9 collective-permute-start.37
  700.5 8.0 collective-permute-start.31
  706.0 9.6 %collective-permute-start.53 = (f32[256,16]{0,1:T(8,128)S(1)}, f32[256,16]{0,1:T(8,128)S(1)}, u32[]{:S(2)}, u32[]{:S(2)}) collective-permute-start(f32[256,16]{0,1:T(8,128)S(1)} %maximum_select_fusion.57), channel_id=1, source_target_pairs={{0,16},{16,0},{2,18},{18,2},{4,20},{20,4},{6,22},{22,6},{8,24},{24... | collective-permute-start | bytes 49160 | tf_op jit(solution)/shard_map/ppermute | solution.py:27
  708.5 44.7 %collective-permute-start.45 = (f32[256,16]{0,1:T(8,128)S(1)}, f32[256,16]{0,1:T(8,128)S(1)}, u32[]{:S(2)}, u32[]{:S(2)}) collective-permute-start(f32[256,16]{0,1:T(8,128)S(1)} %maximum_select_fusion.56), channel_id=1, source_target_pairs={{0,16},{16,0},{2,18},{18,2},{4,20},{20,4},{6,22},{22,6},{8,24},{24... | collective-permute-start | bytes 49160 | tf_op jit(solution)/shard_map/ppermute | solution.py:27
  710.6 39.4 %collective-permute-start.47 = (bf16[64,16,128]{2,1,0:T(8,128)(2,1)S(1)}, bf16[64,16,128]{2,1,0:T(8,128)(2,1)S(1)}, u32[]{:S(2)}, u32[]{:S(2)}) collective-permute-start(bf16[64,16,128]{2,1,0:T(8,128)(2,1)S(1)} %maximum_select_fusion.45), channel_id=1, source_target_pairs={{0,4},{4,0},{2,6},{6,2},{8,12},{12,8},{10,14},{14,10},{16,20},{20,... | collective-permute-start | bytes 786440 | tf_op jit(solution)/shard_map/ppermute | solution.py:27
  715.3 85.7 %collective-permute-start.23 = (bf16[256,16,128]{0,2,1:T(8,128)(2,1)S(1)}, bf16[256,16,128]{0,2,1:T(8,128)(2,1)}, u32[]{:S(2)}, u32[]{:S(2)}) collective-permute-start(bf16[256,16,128]{0,2,1:T(8,128)(2,1)S(1)} %maximum_select_fusion.19), channel_id=1, source_target_pairs={{0,4},{4,0},{2,6},{6,2},{8,12},{12,8},{10,14},{14,10},{16,20},{20,... | collective-permute-start | bytes 3145736 | tf_op jit(solution)/shard_map/ppermute | solution.py:27
  716.7 77.6 %collective-permute-start.33 = (bf16[128,16,128]{2,1,0:T(8,128)(2,1)S(1)}, bf16[128,16,128]{2,1,0:T(8,128)(2,1)S(1)}, u32[]{:S(2)}, u32[]{:S(2)}) collective-permute-start(bf16[128,16,128]{2,1,0:T(8,128)(2,1)S(1)} %maximum_select_fusion.29), channel_id=1, source_target_pairs={{0,4},{4,0},{2,6},{6,2},{8,12},{12,8},{10,14},{14,10},{16,20},{20,... | collective-permute-start | bytes 1572872 | tf_op jit(solution)/shard_map/ppermute | solution.py:27
  750.1 49.2 %collective-permute-start.48 = (bf16[128,16,128]{2,1,0:T(8,128)(2,1)S(1)}, bf16[128,16,128]{2,1,0:T(8,128)(2,1)S(1)}, u32[]{:S(2)}, u32[]{:S(2)}) collective-permute-start(bf16[128,16,128]{2,1,0:T(8,128)(2,1)S(1)} %maximum_select_fusion.31), channel_id=1, source_target_pairs={{0,8},{8,0},{2,10},{10,2},{4,12},{12,4},{6,14},{14,6},{16,24},{24,... | collective-permute-start | bytes 1572872 | tf_op jit(solution)/shard_map/ppermute | solution.py:27
  795.5 58.3 %collective-permute-start.34 = (bf16[256,16,128]{2,1,0:T(8,128)(2,1)}, bf16[256,16,128]{2,1,0:T(8,128)(2,1)}, u32[]{:S(2)}, u32[]{:S(2)}) collective-permute-start(bf16[256,16,128]{2,1,0:T(8,128)(2,1)} %maximum_select_fusion.21), channel_id=1, source_target_pairs={{0,8},{8,0},{2,10},{10,2},{4,12},{12,4},{6,14},{14,6},{16,24},{24,... | collective-permute-start | bytes 3145736 | tf_op jit(solution)/shard_map/ppermute | solution.py:27
  799.5 69.7 %collective-permute-start.49 = (bf16[256,16,128]{2,1,0:T(8,128)(2,1)S(1)}, bf16[256,16,128]{2,1,0:T(8,128)(2,1)}, u32[]{:S(2)}, u32[]{:S(2)}) collective-permute-start(bf16[256,16,128]{2,1,0:T(8,128)(2,1)S(1)} %maximum_select_fusion.23), channel_id=1, source_target_pairs={{0,16},{16,0},{2,18},{18,2},{4,20},{20,4},{6,22},{22,6},{8,24},{24... | collective-permute-start | bytes 3145736 | tf_op jit(solution)/shard_map/ppermute | solution.py:27
  (71 other events, 1547.1 us)
where the time goes:
time: 899 us; the launch traced here: 886 us
  waiting for transfers between devices  525 us (58%)
  starting transfers between devices  123 us (14%)
  local copies, waits for them, and re-layouts  84.6 us (9%)
  other arithmetic  79.2 us (9%)
  matrix products  67.3 us (7%)
    ppermute x54, waiting for transfers between devices, from_partner(): return lax.ppermute(block, axis, route)  525 us
    ppermute x54, starting transfers between devices, from_partner(): return lax.ppermute(block, axis, route)  123 us
    select_n x44, other arithmetic, doubling(): jnp.where(is_lower, jnp.concatenate([own_part, peer_part], 0), jnp.concat...  43.5 us
    broadcast_in_dim x39, local copies, waits for them, and re-layouts, put_rows(): jnp.where(chosen, picked[:, None], jnp.asarray(filler, picked.dtype))  23.9 us
  transfers between devices with their start and end apart: 54, of which 22 were waited for; matrix products, arithmetic and copies ran while one was open for 24% of the time, Pallas kernels for 0%

commit v1 on v0

--- a/solution.py
+++ b/solution.py
@@ -1,4 +1,4 @@
-from functools import reduce
+from functools import partial, reduce
 import math
 
 import jax
@@ -11,20 +11,6 @@
 
 NEG_FILL = -1e30
 EPSILON = 1e-05
-
-
-def as_sent(x):
-    return jax.tree.map(lambda a: a.astype(jnp.bfloat16) if a.dtype == jnp.float32 else a, x)
-
-
-def from_partner(block, axis, stride):
-    count = lax.axis_size(axis)
-    route = []
-    for low in range(count):
-        high = low | 1 << stride
-        if high != low and high < count:
-            route += [(low, high), (high, low)]
-    return lax.ppermute(block, axis, route)
 
 
 def pick_rows(source, mask_table, stride):
@@ -40,41 +26,10 @@
     return spread.reshape((picked.shape[0] * stride,) + picked.shape[1:])
 
 
-def swap_keys(members, bit_num):
-    return jax.tree.map(
-        lambda part, own: part.astype(own.dtype),
-        from_partner(as_sent(members), "ctx", bit_num),
-        members,
-    )
-
-
-def swap_queries(members, bit_num):
-    return jax.tree.map(
-        lambda part, own: part.astype(own.dtype),
-        from_partner(as_sent(members), "ctx", bit_num),
-        members,
-    )
-
-
-def swap_stats(members, bit_num):
-    return from_partner(members, "ctx", bit_num)
-
-
-def doubling(members, group_bits, mover, ctx_index):
-    for bit_num in range(group_bits):
-        arrived = mover(members, bit_num)
-        is_lower = ctx_index >> bit_num & 1 == 0
-        members = tuple(
-            (
-                jnp.where(
-                    is_lower,
-                    jnp.concatenate([own_part, peer_part], 0),
-                    jnp.concatenate([peer_part, own_part], 0),
-                )
-                for own_part, peer_part in zip(members, arrived)
-            )
-        )
-    return members
+def gather_group(members, group_axes):
+    if not group_axes:
+        return members
+    return tuple(lax.all_gather(part, group_axes, axis=0, tiled=True) for part in members)
 
 
 def grad_block(
@@ -109,13 +64,12 @@
     return (query_part, key_part, value_part)
 
 
-def on_device(queries, key_rows, value_rows, offsets, sublayer_norm_gain, cotangent):
+def on_device(queries, key_rows, value_rows, offsets, sublayer_norm_gain, cotangent, level_axes):
     tok_rows = queries.shape[0]
     head_local = offsets.shape[1]
     head_size = queries.shape[1] // head_local
     level_count = offsets.shape[0]
     feature_total_count = lax.axis_size("head") * queries.shape[1]
-    ctx_index = lax.axis_index("ctx")
     score_scale = 1.0 / math.sqrt(head_size)
     shape3 = (tok_rows, head_local, head_size)
     query_all = queries.reshape(shape3)
@@ -125,8 +79,7 @@
     def level_layout(level_num):
         stride = 2**level_num
         picked_rows = tok_rows // stride
-        group_size = max(1, SEG0 * stride // tok_rows)
-        group_bits = group_size.bit_length() - 1
+        group_bits = level_axes[level_num]
         seg_count = max(1, picked_rows // SEG0)
         mask_table = jnp.arange(stride, dtype=jnp.int32)[:, None] == offsets[level_num][None, :]
         return (stride, picked_rows, group_bits, seg_count, mask_table)
@@ -140,7 +93,7 @@
         query_sel = pick_rows(query_all, mask_table, stride)
         key_sel = pick_rows(key_all, mask_table, stride)
         value_sel = pick_rows(value_all, mask_table, stride)
-        key_group, value_group = doubling((key_sel, value_sel), group_bits, swap_keys, ctx_index)
+        key_group, value_group = gather_group((key_sel, value_sel), group_bits)
         stored.append((key_group, value_group))
         query_seg = query_sel.reshape(seg_count, -1, head_local, head_size)
         key_seg = key_group.reshape(seg_count, SEG0, head_local, head_size)
@@ -228,10 +181,9 @@
         query_part, unused_key, unused_value = grad_block(
             query_seg, key_seg, value_seg, dout_seg, lse_seg, delta_seg, score_scale, True, False
         )
-        query_group, dout_group = doubling(
-            (query_sel, dout_sel), group_bits, swap_queries, ctx_index
-        )
-        lse_group, delta_group = doubling((lse_sel, delta_sel), group_bits, swap_stats, ctx_index)
+        query_group, dout_group, lse_group, delta_group = gather_group(
+            (query_sel, dout_sel, lse_sel, delta_sel), group_bits
+        )
         unused_query, key_part, value_part = grad_block(
             query_group.reshape(seg_count, SEG0, head_local, head_size),
             key_sel.reshape(seg_count, -1, head_local, head_size),
@@ -257,16 +209,43 @@
     return (normed, query_grad, key_grad, value_grad)
 
 
+def split_mesh(mesh, tok_rows, level_count):
+    ctx_count = mesh.shape["ctx"]
+    sizes = sorted({max(1, SEG0 * 2**level_num // tok_rows) for level_num in range(level_count)})
+    factors = []
+    done = 1
+    for size in sizes:
+        if size > done:
+            factors.append(size // done)
+            done = size
+    factors.append(ctx_count // done)
+    names = tuple(f"c{index}" for index in range(len(factors)))
+    shape = tuple(reversed(factors)) + (mesh.shape["head"],)
+    sub_mesh = jax.sharding.Mesh(
+        mesh.devices.reshape(shape), tuple(reversed(names)) + ("head",)
+    )
+    level_axes = []
+    for level_num in range(level_count):
+        size = max(1, SEG0 * 2**level_num // tok_rows)
+        count = 0
+        span = 1
+        while span < size:
+            span *= factors[count]
+            count += 1
+        level_axes.append(tuple(reversed(names[:count])))
+    return sub_mesh, tuple(reversed(names)), level_axes
+
+
 def solution(mesh):
-    in_specs = (
-        P("ctx", "head"),
-        P("ctx", "head"),
-        P("ctx", "head"),
-        P(None, "head"),
-        P("head"),
-        P("ctx", "head"),
-    )
-    out_specs = (P("ctx", "head"), P("ctx", "head"), P("ctx", "head"), P("ctx", "head"))
-    return jax.shard_map(
-        on_device, mesh=mesh, in_specs=in_specs, out_specs=out_specs, check_vma=False
-    )
+    def run(queries, key_rows, value_rows, offsets, sublayer_norm_gain, cotangent):
+        tok_rows = queries.shape[0] // mesh.shape["ctx"]
+        sub_mesh, ctx_axes, level_axes = split_mesh(mesh, tok_rows, offsets.shape[0])
+        rows = P(ctx_axes, "head")
+        in_specs = (rows, rows, rows, P(None, "head"), P("head"), rows)
+        out_specs = (rows, rows, rows, rows)
+        body = partial(on_device, level_axes=level_axes)
+        return jax.shard_map(
+            body, mesh=sub_mesh, in_specs=in_specs, out_specs=out_specs, check_vma=False
+        )(queries, key_rows, value_rows, offsets, sublayer_norm_gain, cotangent)
+
+    return run

time: 899 us -> 707 us (0.79)
  waiting for transfers between devices: 525 us -> 328 us
  blocking collectives: 5.42 us -> 148 us
  starting transfers between devices: 123 us -> 0.87 us
  other arithmetic: 79.2 us -> 33.2 us
  local copies, waits for them, and re-layouts: 84.6 us -> 109 us
  between operations: 2.05 us -> 15.5 us
    ppermute x54 -> x0, waiting for transfers between devices: 525 us -> none  [from_partner(): return lax.ppermute(block, axis, route)]
    all_gather x0 -> x12, waiting for transfers between devices: none -> 326 us  [gather_group(): lax.all_gather(part, group_axes, axis=0, tiled=True)]
    all_gather x0 -> x6, blocking collectives: none -> 142 us  [gather_group(): lax.all_gather(part, group_axes, axis=0, tiled=True)]
    ppermute x54 -> x0, starting transfers between devices: 123 us -> none  [from_partner(): return lax.ppermute(block, axis, route)]
    select_n x44 -> x0, other arithmetic: 43.5 us -> none  [doubling(): jnp.where(is_lower, jnp.concatenate([own_part, peer_part], 0), jnp.concat...]
    unnamed x141 -> x128, local copies, waits for them, and re-layouts: 10.7 us -> 24.1 us
    broadcast_in_dim x39 -> x45, local copies, waits for them, and re-layouts: 23.9 us -> 36.9 us  [put_rows(): jnp.where(chosen, picked[:, None], jnp.asarray(filler, picked.dtype))]
    mul x6 -> x0, local copies, waits for them, and re-layouts: 11.2 us -> none  [the longest x4 7.62 us: on_device(): summed = summed + factors[level_num][..., None] * partials[level_num]]
  transfers between devices with their start and end apart: 54 -> 12, of which waited for: 22 -> 8; matrix products, arithmetic and copies ran while one was open for 24% -> 26% of each run, Pallas kernels for 0% -> 0%
where the time goes in v1:
time: 707 us; the launch traced here: 701 us
  waiting for transfers between devices  328 us (46%)
  blocking collectives  148 us (21%)
  local copies, waits for them, and re-layouts  109 us (15%)
  matrix products  66.8 us (9%)
  other arithmetic  33.2 us (5%)
  between operations  15.5 us (2%)
    all_gather x12, waiting for transfers between devices, gather_group(): lax.all_gather(part, group_axes, axis=0, tiled=True)  326 us
    all_gather x6, blocking collectives, gather_group(): lax.all_gather(part, group_axes, axis=0, tiled=True)  142 us
    broadcast_in_dim x45, local copies, waits for them, and re-layouts, put_rows(): jnp.where(chosen, picked[:, None], jnp.asarray(filler, picked.dtype))  36.9 us
    unnamed x128, local copies, waits for them, and re-layouts  24.1 us
    dot_general x3, matrix products, grad_block(): jnp.einsum('shqk,sqhd->skhd', dscores, query_seg, preferred_element_type=...  14.4 us
  transfers between devices with their start and end apart: 12, of which 8 were waited for; matrix products, arithmetic and copies ran while one was open for 26% of the time, Pallas kernels for 0%

profile of v1, /device:TPU:2, one launch (start us, length us, event | category | flops | bytes accessed | tf_op | source)
XLA Modules:
  0.0 701.0 jit_solution(9627745844129497146)
XLA Ops:
  24.1 41.0 %all-gather.17.cloned.1.call-done = bf16[512,16,128]{2,0,1:T(8,128)(2,1)} async-done(((bf16[128,16,128]{2,0,1:T(8,128)(2,1)}), bf16[512,16,128]{2,0,1:T(8,128)(2,1)}) %all-gather.17.cloned.1.call-update) | async-done | bytes 2097168 | tf_op jit(solution)/shard_map/all_gather | solution.py:32
  65.1 2.4 multiply_reduce_fusion
  67.5 1.9 copy-done
  71.4 36.1 %all-gather.19.cloned.1.call-done = bf16[512,16,128]{2,0,1:T(8,128)(2,1)} async-done(((bf16[64,16,128]{2,0,1:T(8,128)(2,1)}), bf16[512,16,128]{2,0,1:T(8,128)(2,1)}) %all-gather.19.cloned.1.call-update) | async-done | bytes 2097168 | tf_op jit(solution)/shard_map/all_gather | solution.py:32
  107.4 2.5 multiply_reduce_fusion.1
  112.7 36.0 %all-gather.25.cloned.1.call-done = bf16[512,16,128]{2,0,1:T(8,128)(2,1)} async-done(((bf16[64,16,128]{2,0,1:T(8,128)(2,1)}), bf16[512,16,128]{2,0,1:T(8,128)(2,1)}) %all-gather.25.cloned.1.call-update) | async-done | bytes 2097168 | tf_op jit(solution)/shard_map/all_gather | solution.py:32
  148.7 2.2 convolution_bitcast_fusion.1
  153.1 66.3 %all-gather.21.cloned.1.call-done = bf16[512,16,128]{2,0,1:T(8,128)(2,1)} async-done(((bf16[32,16,128]{2,0,1:T(8,128)(2,1)}), bf16[512,16,128]{2,0,1:T(8,128)(2,1)}) %all-gather.21.cloned.1.call-update) | async-done | bytes 2097168 | tf_op jit(solution)/shard_map/all_gather | solution.py:32
  219.3 2.6 fusion.116
  230.0 59.6 %all-gather.27.cloned.1.call-done = bf16[512,16,128]{2,0,1:T(8,128)(2,1)} async-done(((bf16[32,16,128]{2,0,1:T(8,128)(2,1)}), bf16[512,16,128]{2,0,1:T(8,128)(2,1)}) %all-gather.27.cloned.1.call-update) | async-done | bytes 2097168 | tf_op jit(solution)/shard_map/all_gather | solution.py:32
  289.6 2.1 convolution_bitcast_fusion.3
  293.2 2.5 copy.275
  297.3 42.7 %all-gather.23.cloned.1.call-done = bf16[512,16,128]{2,0,1:T(8,128)(2,1)} async-done(((bf16[128,16,128]{2,0,1:T(8,128)(2,1)}), bf16[512,16,128]{2,0,1:T(8,128)(2,1)}) %all-gather.23.cloned.1.call-update) | async-done | bytes 2097168 | tf_op jit(solution)/shard_map/all_gather | solution.py:32
  342.8 6.2 convert_reduce_fusion
  349.1 2.5 copy.263
  351.6 3.1 all-reduce.1
  355.4 3.8 fusion.66
  359.2 3.1 all-reduce
  363.1 2.7 multiply_convert_fusion.4
  365.7 2.1 copy.294
  367.8 2.0 broadcast_select_fusion
  369.8 2.1 copy.309
  385.2 6.8 all-gather.29.cloned.1.call-done
  392.0 4.4 fusion.117
  396.4 37.9 %all-gather.33.cloned.1.call-done = bf16[512,16,128]{2,0,1:T(8,128)(2,1)} async-done(((bf16[64,16,128]{2,0,1:T(8,128)(2,1)}), bf16[512,16,128]{2,0,1:T(8,128)(2,1)}) %all-gather.33.cloned.1.call-update) | async-done | bytes 2097168 | tf_op jit(solution)/shard_map/all_gather | solution.py:32
  434.3 3.8 fusion.111
  442.2 2.0 copy.354
  444.2 2.1 fusion.35
  449.3 2.1 fusion.86
  460.0 24.8 %all-gather.1 = f32[8,64,16]{1,2,0:T(8,128)S(1)} all-gather(f32[1,64,16]{1,2,0:T(8,128)} %copy.335), channel_id=1, replica_groups=mesh['c3'=8,'c2'=2,'c1'=2,'c0'=4,'head'=2] {'c1','c0'}, dimensions={0}, use_global_device_ids=true | all-gather | bytes 36864 | tf_op jit(solution)/shard_map/all_gather | solution.py:32
  486.9 24.7 %all-gather = f32[8,64,16]{1,2,0:T(8,128)S(1)} all-gather(f32[1,64,16]{1,2,0:T(8,128)} %copy.331), channel_id=1, replica_groups=mesh['c3'=8,'c2'=2,'c1'=2,'c0'=4,'head'=2] {'c1','c0'}, dimensions={0}, use_global_device_ids=true | all-gather | bytes 36864 | tf_op jit(solution)/shard_map/all_gather | solution.py:32
  515.2 2.4 select_reduce_fusion.9
  526.5 32.2 %all-gather.2 = f32[16,32,16]{1,2,0:T(8,128)S(1)} all-gather(f32[1,32,16]{1,2,0:T(8,128)S(1)} %copy.341), channel_id=1, replica_groups=mesh['c3'=8,'c2'=2,'c1'=2,'c0'=4,'head'=2] {'c2','c1','c0'}, dimensions={0}, use_global_device_ids=true | all-gather | bytes 34816 | tf_op jit(solution)/shard_map/all_gather | solution.py:32
  561.0 31.9 %all-gather.3 = f32[16,32,16]{1,2,0:T(8,128)S(1)} all-gather(f32[1,32,16]{1,2,0:T(8,128)S(1)} %copy.345), channel_id=1, replica_groups=mesh['c3'=8,'c2'=2,'c1'=2,'c0'=4,'head'=2] {'c2','c1','c0'}, dimensions={0}, use_global_device_ids=true | all-gather | bytes 34816 | tf_op jit(solution)/shard_map/all_gather | solution.py:32
  597.8 4.1 fusion.33
  603.7 3.5 fusion.27
  611.1 14.2 %all_gather.61 = f32[512,16]{0,1:T(8,128)} all-gather(f32[128,16]{0,1:T(8,128)} %get-tuple-element.38), channel_id=1, replica_groups=mesh['c3'=8,'c2'=2,'c1'=2,'c0'=4,'head'=2] {'c0'}, dimensions={0}, use_global_device_ids=true | all-gather | bytes 40960 | tf_op jit(solution)/shard_map/all_gather | solution.py:32
  626.0 13.9 %all_gather.63 = f32[512,16]{0,1:T(8,128)} all-gather(f32[128,16]{0,1:T(8,128)S(1)} %broadcast_select_fusion.8), channel_id=1, replica_groups=mesh['c3'=8,'c2'=2,'c1'=2,'c0'=4,'head'=2] {'c0'}, dimensions={0}, use_global_device_ids=true | all-gather | bytes 40960 | tf_op jit(solution)/shard_map/all_gather | solution.py:32
  641.4 2.5 fusion.19
  643.9 6.0 fusion.21
  649.9 5.9 fusion.3
  655.8 6.7 convolution_multiply_fusion.1
  662.6 2.1 convolution_bitcast_fusion
  665.8 4.2 fusion.25
  674.9 2.2 convolution_bitcast_fusion.2
  677.3 3.4 fusion.31
  685.4 4.2 fusion.50
  689.6 2.0 copy.357
  (252 shorter events, 109.9 us)
Async XLA Ops:
  7.2 2.5 copy-start.15
  7.2 58.0 %all-gather.17.cloned.1.call-start = ((), (), s32[]{:S(2)}) async-start(), calls=%async_computation | async-start | bytes 2621440 | tf_op jit(solution)/shard_map/all_gather | solution.py:32
  8.0 13.1 %copy-start.39 = (pred[16]{0:T(512)(128)(4,1)}, pred[16]{0:T(512)(128)(4,1)S(1)}, u32[]{:S(2)}) copy-start(pred[16]{0:T(512)(128)(4,1)S(1)} %compare_bitcast_fusion) | copy-start | bytes 52
  8.0 2.2 copy-start.14
  12.1 95.4 %all-gather.19.cloned.1.call-start = ((), (), s32[]{:S(2)}) async-start(), calls=%async_computation.1 | async-start | bytes 2359296 | tf_op jit(solution)/shard_map/all_gather | solution.py:32
  13.2 9.2 %copy-start.46 = (pred[2,16]{1,0:T(4,128)(4,1)}, pred[2,16]{1,0:T(4,128)(4,1)S(1)}, u32[]{:S(2)}) copy-start(pred[2,16]{1,0:T(4,128)(4,1)S(1)} %iota_compare_fusion.1) | copy-start | bytes 100
  13.9 4.0 copy-start.10
  14.7 133.9 %all-gather.25.cloned.1.call-start = ((), (), s32[]{:S(2)}) async-start(), calls=%async_computation.4 | async-start | bytes 2359296 | tf_op jit(solution)/shard_map/all_gather | solution.py:32
  15.6 203.7 %all-gather.21.cloned.1.call-start = ((), (), s32[]{:S(2)}) async-start(), calls=%async_computation.2 | async-start | bytes 2228224 | tf_op jit(solution)/shard_map/all_gather | solution.py:32
  15.7 6.0 copy-start.47
  15.7 7.5 %copy-start.21 = (bf16[128,2048]{1,0:T(8,128)(2,1)S(1)}, bf16[128,2048]{1,0:T(8,128)(2,1)}, u32[]{:S(2)}) copy-start(bf16[128,2048]{1,0:T(8,128)(2,1)} %param.11) | copy-start | bytes 1572868
  16.3 7.8 %copy-start.17 = (bf16[32,16,128]{2,1,0:T(8,128)(2,1)}, bf16[32,16,128]{2,1,0:T(8,128)(2,1)S(1)}, u32[]{:S(2)}) copy-start(bf16[32,16,128]{2,1,0:T(8,128)(2,1)S(1)} %get-tuple-element.32) | copy-start | bytes 393220
  16.3 7.8 %copy-start.18 = (bf16[32,16,128]{2,1,0:T(8,128)(2,1)}, bf16[32,16,128]{2,1,0:T(8,128)(2,1)S(1)}, u32[]{:S(2)}) copy-start(bf16[32,16,128]{2,1,0:T(8,128)(2,1)S(1)} %get-tuple-element.31) | copy-start | bytes 393220
  16.3 48.8 %copy-start.6 = (bf16[128,16,128]{2,0,1:T(8,128)(2,1)S(1)}, bf16[128,16,128]{2,0,1:T(8,128)(2,1)}, u32[]{:S(2)}) copy-start(bf16[128,16,128]{2,0,1:T(8,128)(2,1)} %get-tuple-element.62) | copy-start | bytes 1572868
  17.1 272.5 %all-gather.27.cloned.1.call-start = ((), (), s32[]{:S(2)}) async-start(), calls=%async_computation.5 | async-start | bytes 2228224 | tf_op jit(solution)/shard_map/all_gather | solution.py:32
  17.9 322.2 %all-gather.23.cloned.1.call-start = ((), (), s32[]{:S(2)}) async-start(), calls=%async_computation.3 | async-start | bytes 2621440 | tf_op jit(solution)/shard_map/all_gather | solution.py:32
  18.4 373.6 %all-gather.29.cloned.1.call-start = ((), (), s32[]{:S(2)}) async-start(), calls=%async_computation.6 | async-start | bytes 2621440 | tf_op jit(solution)/shard_map/all_gather | solution.py:32
  19.2 415.1 %all-gather.33.cloned.1.call-start = ((), (), s32[]{:S(2)}) async-start(), calls=%async_computation.8 | async-start | bytes 2359296 | tf_op jit(solution)/shard_map/all_gather | solution.py:32
  20.0 621.3 %all-gather.37.cloned.1.call-start = ((), (), s32[]{:S(2)}) async-start(), calls=%async_computation.10 | async-start | bytes 2228224 | tf_op jit(solution)/shard_map/all_gather | solution.py:32
  20.8 629.1 %all-gather.31.cloned.1.call-start = ((), (), s32[]{:S(2)}) async-start(), calls=%async_computation.7 | async-start | bytes 2621440 | tf_op jit(solution)/shard_map/all_gather | solution.py:32
  21.7 45.8 %copy-start.27 = (pred[32,4,16]{2,1,0:T(4,128)(4,1)}, pred[32,4,16]{2,1,0:T(4,128)(4,1)S(1)}, u32[]{:S(2)}) copy-start(pred[32,4,16]{2,1,0:T(4,128)(4,1)S(1)} %broadcast_in_dim.468) | copy-start | bytes 6148
  67.5 2.0 copy-start
  67.5 3.8 copy-start.24
  109.9 38.8 %copy-start.23 = (f32[16,64]{1,0:T(8,128)}, f32[16,64]{1,0:T(8,128)S(1)}, u32[]{:S(2)}) copy-start(f32[16,64]{1,0:T(8,128)S(1)} %get-tuple-element.65) | copy-start | bytes 12292
  340.0 2.7 copy-start.12
  340.0 2.8 copy-start.25
  340.0 2.8 copy-start.33
  340.0 2.8 copy-start.34
  340.0 2.8 copy-start.35
  340.0 2.8 copy-start.36
  340.0 2.8 copy-start.40
  340.0 2.8 copy-start.41
  340.1 2.8 copy-start.43
  355.4 3.8 copy-start.48
  355.4 3.8 copy-start.49
  369.8 292.8 %all-gather.35.cloned.1.call-start = ((), (), s32[]{:S(2)}) async-start(), calls=%async_computation.9 | async-start | bytes 2359296 | tf_op jit(solution)/shard_map/all_gather | solution.py:32
  376.3 298.7 %all-gather.39.cloned.1.call-start = ((), (), s32[]{:S(2)}) async-start(), calls=%async_computation.11 | async-start | bytes 2228224 | tf_op jit(solution)/shard_map/all_gather | solution.py:32
  434.3 3.8 copy-start.22
  597.8 6.0 copy-start.31
  597.8 6.0 copy-start.32
  609.4 30.5 %copy-start.26 = (f32[16,128]{1,0:T(8,128)S(1)}, f32[16,128]{1,0:T(8,128)}, u32[]{:S(2)}) copy-start(f32[16,128]{1,0:T(8,128)} %copy-done.24) | copy-start | bytes 24580
  609.4 30.5 %copy-start.29 = (f32[16,128]{1,0:T(8,128)S(1)}, f32[16,128]{1,0:T(8,128)}, u32[]{:S(2)}) copy-start(f32[16,128]{1,0:T(8,128)} %fusion) | copy-start | bytes 24580
  611.1 32.8 %copy-start.2 = (bf16[512,16,128]{2,0,1:T(8,128)(2,1)S(1)}, bf16[512,16,128]{2,0,1:T(8,128)(2,1)}, u32[]{:S(2)}) copy-start(bf16[512,16,128]{2,0,1:T(8,128)(2,1)} %all-gather.17.cloned.1.call-done) | copy-start | bytes 6291460
  641.4 2.6 copy-start.37
  641.4 2.6 copy-start.38
  655.8 6.7 copy-start.1
  674.9 2.3 copy-start.3
  683.7 1.7 copy-start.7
  (15 other events, 18.5 us)
Sparse Core Ops, SparseCore 0:
  12.2 52.9 all-gather.16
  66.9 40.4 all-gather.18
  109.2 39.4 all-gather.24
  150.3 68.9 all-gather.20
  221.0 68.5 all-gather.26
  291.8 48.1 all-gather.22
  342.4 49.5 all-gather.28
  393.8 40.4 all-gather.32
  436.1 68.9 all-gather.36
  506.7 49.4 all-gather.30
  558.0 40.7 all-gather.34
  600.5 68.5 all-gather.38

commit v2 on v1

--- a/solution.py
+++ b/solution.py
@@ -29,7 +29,35 @@
 def gather_group(members, group_axes):
     if not group_axes:
         return members
-    return tuple(lax.all_gather(part, group_axes, axis=0, tiled=True) for part in members)
+    stacked = jnp.stack(members, axis=1)
+    whole = lax.all_gather(stacked, group_axes, axis=0, tiled=True)
+    return tuple(whole[:, index] for index in range(len(members)))
+
+
+def split_three(values):
+    high = lax.reduce_precision(values, exponent_bits=8, mantissa_bits=7)
+    rest = values - high
+    middle = lax.reduce_precision(rest, exponent_bits=8, mantissa_bits=7)
+    low = rest - middle
+    return jnp.stack([high, middle, low], axis=-1).astype(jnp.bfloat16)
+
+
+def gather_rows(query_sel, dout_sel, lse_sel, delta_sel, group_axes):
+    if not group_axes:
+        return (query_sel, dout_sel, lse_sel, delta_sel)
+    rows = query_sel.shape[0]
+    width = query_sel.shape[1] * query_sel.shape[2]
+    pieces = split_three(jnp.stack([lse_sel, delta_sel], axis=-1))
+    flat = jnp.concatenate(
+        [query_sel.reshape(rows, width), dout_sel.reshape(rows, width), pieces.reshape(rows, -1)], axis=1
+    )
+    whole = lax.all_gather(flat, group_axes, axis=0, tiled=True)
+    count = whole.shape[0]
+    query_group = whole[:, :width].reshape((count,) + query_sel.shape[1:])
+    dout_group = whole[:, width : 2 * width].reshape((count,) + query_sel.shape[1:])
+    parts = whole[:, 2 * width :].reshape((count,) + pieces.shape[1:]).astype(jnp.float32)
+    stats = parts[..., 0] + parts[..., 1] + parts[..., 2]
+    return (query_group, dout_group, stats[..., 0], stats[..., 1])
 
 
 def grad_block(
@@ -181,8 +209,8 @@
         query_part, unused_key, unused_value = grad_block(
             query_seg, key_seg, value_seg, dout_seg, lse_seg, delta_seg, score_scale, True, False
         )
-        query_group, dout_group, lse_group, delta_group = gather_group(
-            (query_sel, dout_sel, lse_sel, delta_sel), group_bits
+        query_group, dout_group, lse_group, delta_group = gather_rows(
+            query_sel, dout_sel, lse_sel, delta_sel, group_bits
         )
         unused_query, key_part, value_part = grad_block(
             query_group.reshape(seg_count, SEG0, head_local, head_size),

time: 707 us -> 571 us (0.81)
  blocking collectives: 148 us -> 6.44 us
  local copies, waits for them, and re-layouts: 109 us -> 131 us
  waiting for transfers between devices: 328 us -> 315 us
  matrix products: 66.8 us -> 57.1 us
    all_gather x6 -> x0, blocking collectives: 142 us -> none  [gather_group(): lax.all_gather(part, group_axes, axis=0, tiled=True)]
    unnamed x128 -> x159, local copies, waits for them, and re-layouts: 24.1 us -> 44.2 us
    slice x0 -> x5, local copies, waits for them, and re-layouts: none -> 14.1 us  [the longest x3 12.2 us: gather_rows(): whole[:, width:2 * width].reshape((count,) + query_sel.shape[1:])]
    all_gather x12 -> x6, waiting for transfers between devices: 326 us -> 314 us  [the longest x3 192 us: gather_group(): whole = lax.all_gather(stacked, group_axes, axis=0, tiled=True)]
    reshape x8 -> x0, local copies, waits for them, and re-layouts: 10.7 us -> none  [the longest x2 3.14 us: on_device(): delta_group.reshape(seg_count, SEG0, head_local)]
    convert_element_type x0 -> x8, local copies, waits for them, and re-layouts: none -> 7.31 us  [the longest x5 7.03 us: split_three(): return jnp.stack([high, middle, low], axis=-1).astype(jnp.bfloat16)]
    broadcast_in_dim x45 -> x47, local copies, waits for them, and re-layouts: 36.9 us -> 38.8 us  [put_rows(): jnp.where(chosen, picked[:, None], jnp.asarray(filler, picked.dtype))]
  transfers between devices with their start and end apart: 12 -> 6, of which waited for: 8 -> 6; matrix products, arithmetic and copies ran while one was open for 26% -> 21% of each run, Pallas kernels for 0% -> 0%
where the time goes in v2:
time: 571 us; the launch traced here: 564 us
  waiting for transfers between devices  315 us (55%)
  local copies, waits for them, and re-layouts  131 us (23%)
  matrix products  57.1 us (10%)
  other arithmetic  38.5 us (7%)
  between operations  15.5 us (3%)
  blocking collectives  6.44 us (1%)
    all_gather x3, waiting for transfers between devices, gather_group(): whole = lax.all_gather(stacked, group_axes, axis=0, tiled=True)  192 us
    all_gather x3, waiting for transfers between devices, gather_rows(): whole = lax.all_gather(flat, group_axes, axis=0, tiled=True)  122 us
    unnamed x159, local copies, waits for them, and re-layouts  44.2 us
    broadcast_in_dim x47, local copies, waits for them, and re-layouts, put_rows(): jnp.where(chosen, picked[:, None], jnp.asarray(filler, picked.dtype))  38.8 us
    dot_general x3, matrix products, grad_block(): jnp.einsum('shqk,skhd->sqhd', dscores, key_seg, preferred_element_type=jn...  14.2 us
    dot_general x3, matrix products, grad_block(): jnp.einsum('shqk,sqhd->skhd', dscores, query_seg, preferred_element_type=...  13.3 us
    slice x3, local copies, waits for them, and re-layouts, gather_rows(): whole[:, width:2 * width].reshape((count,) + query_sel.shape[1:])  12.2 us
  transfers between devices with their start and end apart: 6, of which 6 were waited for; matrix products, arithmetic and copies ran while one was open for 21% of the time, Pallas kernels for 0%

profile of v2, /device:TPU:2, one launch (start us, length us, event | category | flops | bytes accessed | tf_op | source)
XLA Modules:
  0.0 564.0 jit_solution(1603647679068662094)
XLA Ops:
  22.1 78.0 %all-gather.7.cloned.1.call-done = bf16[512,2,16,128]{3,0,2,1:T(8,128)(2,1)} async-done(((bf16[128,2,16,128]{3,0,2,1:T(8,128)(2,1)}), bf16[512,2,16,128]{3,0,2,1:T(8,128)(2,1)}) %all-gather.7.cloned.1.call-update) | async-done | bytes 4194320 | tf_op jit(solution)/shard_map/all_gather | solution.py:33
  100.1 2.5 multiply_reduce_fusion
  106.2 51.2 %all-gather.9.cloned.1.call-done = bf16[512,2,16,128]{3,0,2,1:T(8,128)(2,1)} async-done(((bf16[64,2,16,128]{3,0,2,1:T(8,128)(2,1)}), bf16[512,2,16,128]{3,0,2,1:T(8,128)(2,1)}) %all-gather.9.cloned.1.call-update) | async-done | bytes 4194320 | tf_op jit(solution)/shard_map/all_gather | solution.py:33
  157.4 2.5 multiply_reduce_fusion.1
  162.7 2.2 fusion.37
  166.6 2.5 copy.782
  170.6 63.1 %all-gather.11.cloned.1.call-done = bf16[512,2,16,128]{3,0,2,1:T(8,128)(2,1)} async-done(((bf16[32,2,16,128]{3,0,2,1:T(8,128)(2,1)}), bf16[512,2,16,128]{3,0,2,1:T(8,128)(2,1)}) %all-gather.11.cloned.1.call-update) | async-done | bytes 4194320 | tf_op jit(solution)/shard_map/all_gather | solution.py:33
  233.7 2.5 fusion.164
  250.2 1.5 copy.791
  251.7 2.1 fusion.42
  256.4 2.6 copy.785
  258.9 2.5 copy.793
  262.3 6.7 %convert_reduce_fusion = (f32[128]{0:T(128)}, f32[128]{0:T(128)}, bf16[128,16,128]{0,2,1:T(8,128)(2,1)}, f32[16,128,128]{2,1,0:T(8,128)}) fusion(f32[128,16]{0,1:T(8,128)S(1)} %get-tuple-element.42, f32[128,16,128]{0,2,1:T(8,128)} %copy.793, pred[128,16]{0,1:T(8,128)(4,1)} %copy.777, f32[128,16]{0,1:T(8,128)S(1)} %get-tuple-element.44, ...), kind=kOutput, calls=%fused_computation.48 | convolution fusion | flops 275250944 | bytes 10008064 | tf_op jit(solution)/shard_map/shqk,skhd->sqhd/dot_general | solution.py:136
  269.0 3.1 all-reduce.1
  272.8 3.7 fusion.77
  276.5 3.3 all-reduce
  280.6 2.8 broadcast_select_fusion.2
  286.3 1.5 copy.820
  287.8 2.1 fusion.129
  293.7 2.4 select_reduce_fusion.9
  296.1 1.5 copy.844
  303.5 2.3 pad_maximum_fusion
  305.9 1.7 copy.1006
  307.6 2.0 copy.817
  332.4 1.6 pad_maximum_fusion.4
  334.0 2.2 multiply_convert_fusion.5
  336.2 2.0 copy.886
  341.8 4.1 fusion.44
  347.1 3.5 fusion.39
  354.6 6.6 %fusion.31 = f32[16,128,128]{2,1,0:T(8,128)} fusion(f32[16,128,512]{2,1,0:T(8,128)} %copy-done.2, f32[16,128]{1,0:T(8,128)S(1)} %get-tuple-element.80, f32[16,128]{1,0:T(8,128)S(1)} %get-tuple-element.79, bf16[512,2,16,128]{3,0,2,1:T(8,128)(2,1)} %all-gather.7.cloned.1.call-done, bf16[128,16,128]{0,2,1:T(8,128)(2,1)S(1)} %bitcast.597, ...), kind=kOutput, calls=%fused_computation.59 | convolution fusion | flops 542638080 | bytes 9977872 | tf_op jit(solution)/shard_map/shqk,skhd->sqhd/dot_general | solution.py:80
  361.2 31.5 %all-gather.13.cloned.1.call-done = bf16[512,4192]{0,1:T(8,128)(2,1)} async-done(((bf16[128,4192]{0,1:T(8,128)(2,1)}), bf16[512,4192]{0,1:T(8,128)(2,1)}) %all-gather.13.cloned.1.call-update) | async-done | bytes 4292624 | tf_op jit(solution)/shard_map/all_gather | solution.py:54
  394.0 2.6 fusion.163
  397.8 3.8 fusion.3
  401.6 7.1 %convolution_multiply_fusion.1 = f32[16,128,128]{2,1,0:T(8,128)} fusion(bf16[512,16,128]{0,2,1:T(8,128)(2,1)} %bitcast.588, f32[16,512,128]{2,1,0:T(8,128)} %copy-done.1, bf16[512,16,128]{0,2,1:T(8,128)(2,1)S(1)} %bitcast.586, f32[16,512]{1,0:T(8,128)S(1)} %bitcast.678, f32[16,512]{1,0:T(8,128)S(1)} %bitcast.663, bf16[128,16,128]{0,2,1:T(8,128)(2,1)S(1)} %bitcast.620, ...), kind=kOutput, calls=%fused_computation.54 | convolution fusion | flops 542638080 | bytes 10027024 | tf_op jit(solution)/shard_map/shqk,sqhd->skhd/dot_general | solution.py:86
  408.7 38.9 %all-gather.15.cloned.1.call-done = bf16[512,4192]{1,0:T(8,128)(2,1)} async-done(((bf16[64,4192]{1,0:T(8,128)(2,1)}), bf16[512,4192]{1,0:T(8,128)(2,1)}) %all-gather.15.cloned.1.call-update) | async-done | bytes 4292624 | tf_op jit(solution)/shard_map/all_gather | solution.py:54
  448.6 4.8 fusion.162
  453.4 2.9 copy.920
  456.6 4.0 copy.919
  460.6 2.0 fusion.115
  464.3 3.5 fusion.35
  471.7 51.8 %all-gather.17.cloned.1.call-done = bf16[512,4192]{1,0:T(8,128)(2,1)} async-done(((bf16[32,4192]{1,0:T(8,128)(2,1)}), bf16[512,4192]{1,0:T(8,128)(2,1)}) %all-gather.17.cloned.1.call-update) | async-done | bytes 4292624 | tf_op jit(solution)/shard_map/all_gather | solution.py:54
  524.6 4.9 fusion.161
  529.4 2.9 copy.922
  533.3 4.2 copy.921
  537.5 2.0 fusion.28
  541.0 2.7 fusion.41
  548.6 4.2 fusion.61
  552.9 2.0 copy.889
  (283 shorter events, 106.3 us)
Async XLA Ops:
  7.2 93.0 %all-gather.7.cloned.1.call-start = ((), (), s32[]{:S(2)}) async-start(), calls=%async_computation | async-start | bytes 5242880 | tf_op jit(solution)/shard_map/all_gather | solution.py:33
  7.9 92.2 %copy-start.41 = (pred[16]{0:T(512)(128)(4,1)}, pred[16]{0:T(512)(128)(4,1)S(1)}, u32[]{:S(2)}) copy-start(pred[16]{0:T(512)(128)(4,1)S(1)} %compare_bitcast_fusion) | copy-start | bytes 52
  9.2 2.8 copy-start.8
  13.1 144.3 %all-gather.9.cloned.1.call-start = ((), (), s32[]{:S(2)}) async-start(), calls=%async_computation.1 | async-start | bytes 4718592 | tf_op jit(solution)/shard_map/all_gather | solution.py:33
  14.3 5.5 copy-start.55
  15.0 1.7 copy-start.14
  15.0 142.5 %copy-start.13 = (bf16[64,16,128]{2,1,0:T(8,128)(2,1)}, bf16[64,16,128]{2,1,0:T(8,128)(2,1)S(1)}, u32[]{:S(2)}) copy-start(bf16[64,16,128]{2,1,0:T(8,128)(2,1)S(1)} %get-tuple-element.28) | copy-start | bytes 786436
  16.0 217.7 %all-gather.11.cloned.1.call-start = ((), (), s32[]{:S(2)}) async-start(), calls=%async_computation.2 | async-start | bytes 4456448 | tf_op jit(solution)/shard_map/all_gather | solution.py:33
  16.1 2.4 copy-start.56
  16.7 85.9 %copy-start.21 = (bf16[32,16,128]{2,1,0:T(8,128)(2,1)}, bf16[32,16,128]{2,1,0:T(8,128)(2,1)S(1)}, u32[]{:S(2)}) copy-start(bf16[32,16,128]{2,1,0:T(8,128)(2,1)S(1)} %get-tuple-element.33) | copy-start | bytes 393220
  16.7 85.9 %copy-start.23 = (bf16[32,16,128]{2,1,0:T(8,128)(2,1)}, bf16[32,16,128]{2,1,0:T(8,128)(2,1)S(1)}, u32[]{:S(2)}) copy-start(bf16[32,16,128]{2,1,0:T(8,128)(2,1)S(1)} %get-tuple-element.32) | copy-start | bytes 393220
  16.7 3.8 copy-start.31
  17.6 375.1 %all-gather.13.cloned.1.call-start = ((), (), s32[]{:S(2)}) async-start(), calls=%async_computation.3 | async-start | bytes 5365760 | tf_op jit(solution)/shard_map/all_gather | solution.py:54
  18.4 84.2 %copy-start.10 = (bf16[128,2048]{0,1:T(8,128)(2,1)}, bf16[128,2048]{0,1:T(8,128)(2,1)S(1)}, u32[]{:S(2)}) copy-start(bf16[128,2048]{0,1:T(8,128)(2,1)S(1)} %copy.760) | copy-start | bytes 1572868
  102.6 2.0 copy-start.2
  104.8 55.2 %copy-start.29 = (f32[1,128,16]{2,1,0:T(8,128)}, f32[1,128,16]{2,1,0:T(8,128)S(1)}, u32[]{:S(2)}) copy-start(f32[1,128,16]{2,1,0:T(8,128)S(1)} %copy.810) | copy-start | bytes 24580
  105.6 54.4 %copy-start.30 = (f32[1,128,16]{2,1,0:T(8,128)}, f32[1,128,16]{2,1,0:T(8,128)S(1)}, u32[]{:S(2)}) copy-start(f32[1,128,16]{2,1,0:T(8,128)S(1)} %copy.805) | copy-start | bytes 24580
  262.3 6.7 %copy-start.43 = (f32[128,16]{0,1:T(8,128)}, f32[128,16]{0,1:T(8,128)S(1)}, u32[]{:S(2)}) copy-start(f32[128,16]{0,1:T(8,128)S(1)} %get-tuple-element.42) | copy-start | bytes 24580
  262.3 6.7 %copy-start.44 = (f32[128,16]{0,1:T(8,128)}, f32[128,16]{0,1:T(8,128)S(1)}, u32[]{:S(2)}) copy-start(f32[128,16]{0,1:T(8,128)S(1)} %get-tuple-element.43) | copy-start | bytes 24580
  262.3 6.7 %copy-start.45 = (f32[128,16]{0,1:T(8,128)}, f32[128,16]{0,1:T(8,128)S(1)}, u32[]{:S(2)}) copy-start(f32[128,16]{0,1:T(8,128)S(1)} %get-tuple-element.44) | copy-start | bytes 24580
  262.3 6.7 %copy-start.46 = (f32[128,16]{0,1:T(8,128)}, f32[128,16]{0,1:T(8,128)S(1)}, u32[]{:S(2)}) copy-start(f32[128,16]{0,1:T(8,128)S(1)} %get-tuple-element.45) | copy-start | bytes 24580
  272.8 3.7 copy-start.53
  272.8 3.7 copy-start.54
  279.9 4.3 copy-start.32
  303.5 6.1 %copy-start.47 = (f32[64,16]{0,1:T(8,128)S(1)}, f32[64,16]{0,1:T(8,128)}, u32[]{:S(2)}) copy-start(f32[64,16]{0,1:T(8,128)} %get-tuple-element.26) | copy-start | bytes 12292
  305.8 141.7 %all-gather.15.cloned.1.call-start = ((), (), s32[]{:S(2)}) async-start(), calls=%async_computation.4 | async-start | bytes 4866048 | tf_op jit(solution)/shard_map/all_gather | solution.py:54
  318.2 3.6 copy-start.26
  318.2 3.6 copy-start.40
  321.8 12.2 %copy-start.38 = (f32[2048]{0:T(1024)S(1)}, f32[2048]{0:T(1024)}, u32[]{:S(2)}) copy-start(f32[2048]{0:T(1024)} %param.10) | copy-start | bytes 24580
  322.7 200.9 %all-gather.17.cloned.1.call-start = ((), (), s32[]{:S(2)}) async-start(), calls=%async_computation.5 | async-start | bytes 4595712 | tf_op jit(solution)/shard_map/all_gather | solution.py:54
  323.4 14.8 %copy-start.27 = (f32[64,2,16]{2,1,0:T(2,128)S(1)}, f32[64,2,16]{2,1,0:T(2,128)}, u32[]{:S(2)}) copy-start(f32[64,2,16]{2,1,0:T(2,128)} %copy.794) | copy-start | bytes 24580
  324.9 13.5 %copy-start.28 = (f32[64,2,16]{2,1,0:T(2,128)S(1)}, f32[64,2,16]{2,1,0:T(2,128)}, u32[]{:S(2)}) copy-start(f32[64,2,16]{2,1,0:T(2,128)} %copy.798) | copy-start | bytes 24580
  341.8 5.2 copy-start.48
  341.8 5.2 copy-start.49
  352.8 1.7 copy-start.35
  352.8 1.7 copy-start.37
  352.8 1.7 copy-start.42
  352.8 1.8 copy-start.7
  393.9 2.6 copy-start.9
  397.8 3.8 copy-start.1
  397.8 3.8 copy-start.20
  456.6 4.0 copy-start.15
  533.2 4.2 copy-start.24
  546.9 1.7 copy-start.11
  546.9 1.7 copy-start.12
  546.9 1.7 copy-start.50
  547.0 1.7 copy-start.51
  547.0 1.7 copy-start.52
  (16 other events, 16.0 us)
Sparse Core Ops, SparseCore 0:
  13.2 86.8 all-gather.6
  102.5 54.9 all-gather.8
  159.8 73.8 all-gather.10
  306.0 86.7 all-gather.12
  394.3 53.1 all-gather.14
  449.8 73.7 all-gather.16
